TPU v7x, 32 devices: a whole 2x2x4 slice. The times are simulated.
32 devices in a mesh: groups: 2 (over y), ctx: 4 (over z), head: 4 (over x, core).
Axes of the slice: x: 2, y: 2, z: 4, core: 2. Of those that a mesh axis runs over, the one named last changes fastest.
Arguments:
- hidden_in: bfloat16 [4096, 4096], P(('groups', 'ctx'), 'head'), parts along dimension 0, may hold values from -6 to 6
- attn_gain: float32 [4096], replicated, may hold values from 0.5 to 12, as said below
- w_query: bfloat16 [4096, 2048], P(None, 'head'), may hold values from -0.09375 to 0.09375
- w_keys: bfloat16 [4096, 1024], P(None, 'head'), may hold values from -0.09375 to 0.09375
- w_values: bfloat16 [4096, 1024], P(None, 'head'), may hold values from -0.09375 to 0.09375
- wo_attn: bfloat16 [2048, 4096], P('head'), may hold values from -0.125 to 0.125
- lin_gain: float32 [4096], replicated, may hold values from 0.5 to 1.5
- w_feature: bfloat16 [4096, 256], P(None, 'head'), may hold values from -0.09375 to 0.09375
- wv_linear: bfloat16 [4096, 2048], P(None, 'head'), may hold values from -0.09375 to 0.09375
- out_gain: float32 [8, 256], P('head'), may hold values from 0.5 to 1.5
- wo_linear: bfloat16 [2048, 4096], P('head'), may hold values from -0.125 to 0.125
- entry_state: float32 [16, 273, 256], P(('groups', 'head')), parts along dimension 0, may hold values from -180 to 180
Outputs:
- mixed: bfloat16 [4096, 4096], P(('groups', 'ctx'), 'head'), parts along dimension 0
There are 2 independent parts, one for each index of `groups`. A program takes and returns all parts, laid end to end along the dimension named above; an argument that names none is the same for every part. Nothing has to cross between parts.
Inputs may be any that keep to these rules, and one draw needn't show every extreme that they name: `attn_gain`: a positive gain for every feature.
All inputs are finite; a program needn't handle non-finite values.
Results may differ from a plain program's by a relative error of at most 0.008.
The roundings to bfloat16 on the way count: a program that leaves them out, or rounds other values in their place, can miss the bound.
Values may be sent and summed in bfloat16 or wider, within the bound.
No kernel may reach another device: no remote copies, remote signals or barrier semaphores. Data moves between devices by JAX's collectives and lax.ppermute only.
A program may use at most 128 MiB of HBM per device.

v0:
```python
import math
import jax
import jax.numpy as jnp
from jax import lax
from jax.sharding import PartitionSpec as P

HEAD = 128
WINDOW = 64
FEAT = 16
VDIM = 256


def from_behind(value, axis, by):
    devices = lax.axis_size(axis)
    pairs = [(i, i + by) for i in range(devices) if 0 <= i + by < devices]
    return lax.ppermute(value, axis, pairs)


def norm_rows(values, gain):
    wide = values.astype(jnp.float32)
    scale = lax.rsqrt(jnp.mean(wide * wide, axis=-1, keepdims=True) + 1e-05)
    return (wide * scale * gain).astype(jnp.bfloat16)


def taylor(inputs):
    width = inputs.shape[-1]
    outer = (inputs[..., :, None] * inputs[..., None, :]).reshape(
        inputs.shape[:-1] + (width * width,)
    )
    ones = jnp.ones(inputs.shape[:-1] + (1,), jnp.float32)
    return jnp.concatenate(
        [ones, inputs / width**0.25, outer / (math.sqrt(2.0) * math.sqrt(width))], axis=-1
    )


def body(
    hidden_in,
    attn_gain,
    w_query,
    w_keys,
    w_values,
    wo_attn,
    lin_gain,
    w_feature,
    wv_linear,
    out_gain,
    wo_linear,
    entry_state,
):
    tok_rows = hidden_in.shape[0]
    whole = lax.all_gather(hidden_in, "head", axis=1, tiled=True)
    normed = norm_rows(whole, attn_gain)
    query = jnp.dot(normed, w_query, preferred_element_type=jnp.float32).astype(jnp.bfloat16)
    keys = jnp.dot(normed, w_keys, preferred_element_type=jnp.float32).astype(jnp.bfloat16)
    values = jnp.dot(normed, w_values, preferred_element_type=jnp.float32).astype(jnp.bfloat16)
    kv_cols = keys.shape[1]
    kv_heads = kv_cols // HEAD
    group = query.shape[1] // HEAD // kv_heads
    kv_pair = jnp.concatenate([keys, values], axis=1)
    rim = from_behind(kv_pair[tok_rows - WINDOW :], "ctx", 1)
    kv_all = jnp.concatenate([rim, kv_pair], axis=0)
    key_all = kv_all[:, :kv_cols].reshape(tok_rows + WINDOW, kv_heads, HEAD)
    value_all = kv_all[:, kv_cols:].reshape(tok_rows + WINDOW, kv_heads, HEAD)
    query_heads = query.reshape(tok_rows, kv_heads, group, HEAD)
    scores = jnp.einsum(
        "tkgd,skd->kgts", query_heads, key_all, preferred_element_type=jnp.float32
    ) / math.sqrt(HEAD)
    start = lax.axis_index("ctx") * tok_rows
    qpos = start + jnp.arange(tok_rows, dtype=jnp.int32)
    kpos = start - WINDOW + jnp.arange(tok_rows + WINDOW, dtype=jnp.int32)
    visible = (
        (kpos[None, :] <= qpos[:, None])
        & (kpos[None, :] > qpos[:, None] - WINDOW)
        & (kpos[None, :] >= 0)
    )
    scores = jnp.where(visible, scores, -jnp.inf)
    top = jnp.max(scores, axis=-1, keepdims=True)
    expd = jnp.exp(scores - top)
    probs = (expd / jnp.sum(expd, axis=-1, keepdims=True)).astype(jnp.bfloat16)
    attended = jnp.einsum("kgts,skd->tkgd", probs, value_all, preferred_element_type=jnp.float32)
    attended = attended.astype(jnp.bfloat16).reshape(tok_rows, -1)
    terms = jnp.dot(attended, wo_attn, preferred_element_type=jnp.float32)
    partial_out = lax.psum_scatter(terms, "head", scatter_dimension=1, tiled=True)
    after_window = (hidden_in.astype(jnp.float32) + partial_out).astype(jnp.bfloat16)
    after_whole = lax.all_gather(after_window, "head", axis=1, tiled=True)
    normed2 = norm_rows(after_whole, lin_gain)
    feats = jnp.dot(normed2, w_feature, preferred_element_type=jnp.float32)
    lin_heads = feats.shape[1] // (2 * FEAT)
    feats = feats.reshape(tok_rows, lin_heads, 2, FEAT)
    query_feat = feats[:, :, 0, :]
    key_feat = feats[:, :, 1, :]
    lvalues = (
        jnp.dot(normed2, wv_linear, preferred_element_type=jnp.float32)
        .astype(jnp.bfloat16)
        .reshape(tok_rows, lin_heads, VDIM)
    )
    phi_query = taylor(query_feat)
    phi_key = taylor(key_feat)
    highest = lax.Precision.HIGHEST
    local_state = jnp.einsum(
        "thf,thv->hfv", phi_key, lvalues.astype(jnp.float32), precision=highest
    )
    ctx_count = lax.axis_size("ctx")
    every = (
        lax.all_gather(local_state.astype(jnp.bfloat16), "ctx", axis=0, tiled=True)
        .astype(local_state.dtype)
        .reshape((ctx_count,) + local_state.shape)
    )
    earlier = (jnp.arange(ctx_count, dtype=jnp.int32) < lax.axis_index("ctx")).astype(jnp.float32)
    prior = jnp.einsum("c,chfv->hfv", earlier, every, precision=highest)
    carried = entry_state + prior
    cross = jnp.einsum("thf,hfv->thv", phi_query, carried, precision=highest)
    sims = jnp.einsum("thf,shf->hts", query_feat, key_feat, precision=highest) / math.sqrt(FEAT)
    causal = jnp.arange(tok_rows)[:, None] >= jnp.arange(tok_rows)[None, :]
    weights = jnp.where(causal[None], 1.0 + sims + 0.5 * sims * sims, 0.0).astype(jnp.bfloat16)
    intra = jnp.einsum("hts,shv->thv", weights, lvalues, preferred_element_type=jnp.float32)
    lin_out = cross + intra
    scale = lax.rsqrt(jnp.mean(lin_out * lin_out, axis=-1, keepdims=True) + 1e-05)
    lin_normed = (
        (lin_out * scale * out_gain[None]).astype(jnp.bfloat16).reshape(tok_rows, lin_heads * VDIM)
    )
    lin_terms = jnp.dot(lin_normed, wo_linear, preferred_element_type=jnp.float32)
    lin_part = lax.psum_scatter(lin_terms, "head", scatter_dimension=1, tiled=True)
    return (after_window.astype(jnp.float32) + lin_part).astype(jnp.bfloat16)


def solution(mesh):
    in_specs = (
        P(("groups", "ctx"), "head"),
        P(),
        P(None, "head"),
        P(None, "head"),
        P(None, "head"),
        P("head", None),
        P(),
        P(None, "head"),
        P(None, "head"),
        P("head", None),
        P("head", None),
        P(("groups", "head"), None, None),
    )
    out_specs = P(("groups", "ctx"), "head")
    return jax.shard_map(body, mesh=mesh, in_specs=in_specs, out_specs=out_specs, check_vma=False)
```

profile of v0, /device:TPU:0, one launch (start us, length us, event | category | flops | bytes accessed | tf_op | source)
XLA Modules:
  0.0 315.9 jit_solution(14720713540210426157)
XLA Ops:
  6.5 0.0 copy-start
  6.5 0.0 all-gather.4.cloned.1.call-start
  6.5 0.7 all-gather.4.cloned.1.call-update
  7.3 0.0 reduce-scatter.3.cloned.1.call-start
  7.4 0.3 and_and_fusion
  7.7 38.4 %all-gather.4.cloned.1.call-done = bf16[512,4096]{1,0:T(8,128)(2,1)} async-done(((bf16[512,1024]{1,0:T(8,128)(2,1)}), bf16[512,4096]{1,0:T(8,128)(2,1)}) %all-gather.4.cloned.1.call-update) | async-done | bytes 4194320 | tf_op jit(solution)/shard_map/all_gather | solution.py:51
  46.1 3.2 %fusion.1 = f32[512]{0:T(512)S(1)} fusion(bf16[512,4096]{1,0:T(8,128)(2,1)} %all-gather.4.cloned.1.call-done), kind=kLoop, calls=%fused_computation.5 | loop fusion | flops 6290944 | bytes 4196352 | tf_op jit(solution)/shard_map/reduce_sum | solution.py:21
  49.4 0.0 copy-done
  49.4 0.0 copy-done.15
  49.4 0.2 copy-done.5
  49.6 1.6 convolution_convert_fusion.3
  51.2 0.0 copy-done.13
  51.2 0.0 copy-start.11
  51.2 1.6 convolution_convert_fusion.4
  52.9 0.1 pad_maximum_fusion
  53.0 3.6 %collective-permute-start = (bf16[64,512]{0,1:T(8,128)(2,1)S(1)}, bf16[64,512]{0,1:T(8,128)(2,1)S(1)}, u32[]{:S(2)}, u32[]{:S(2)}) collective-permute-start(bf16[64,512]{0,1:T(8,128)(2,1)S(1)} %pad_maximum_fusion), channel_id=1, source_target_pairs={{0,4},{4,8},{8,12},{1,5},{5,9},{9,13},{2,6},{6,10},{10,14},{3,7},{... | collective-permute-start | bytes 196616 | tf_op jit(solution)/shard_map/ppermute | solution.py:16
  56.6 0.0 copy-done.11
  56.6 2.6 convolution_convert_fusion.1
  59.2 0.3 collective-permute-done
  59.5 0.3 maximum_maximum_fusion
  59.8 0.1 fusion.42
  59.9 3.9 %fusion.43 = (f32[2,2,512]{2,1,0:T(2,128)S(1)}, f32[2,2,512,576]{2,3,1,0:T(8,128)}) fusion(pred[512,576]{0,1:T(8,128)(4,1)S(1)} %and_and_fusion, bf16[576,2,128,1]{0,2,3,1:T(8,128)(2,1)S(1)} %bitcast.82, bf16[512,2,2,128]{0,3,2,1:T(8,128)(2,1)S(1)} %bitcast.84), kind=kOutput, calls=%fused_computation.74 | convolution fusion | flops 306709056 | bytes 5840896 | tf_op jit(solution)/shard_map/sub | solution.py:78
  63.8 3.1 fusion.13
  66.9 0.5 copy-done.3
  67.4 5.7 %fusion.44 = f32[512,4096]{1,0:T(8,128)} fusion(bf16[512,512]{0,1:T(8,128)(2,1)S(1)} %bitcast.75, bf16[512,4096]{1,0:T(8,128)(2,1)S(1)} %copy-done.3), kind=kOutput, calls=%fused_computation.75 | convolution fusion | flops 2147483648 | bytes 13107200 | tf_op jit(solution)/shard_map/dot_general | solution.py:82
  73.1 0.0 reduce-scatter.3.cloned.1.call-update
  73.2 0.0 copy-start.14
  73.2 0.0 copy-start.16
  73.2 0.0 all-gather.6.cloned.1.call-start
  73.2 72.8 %reduce-scatter.3.cloned.1.call-done = f32[512,1024]{1,0:T(8,128)} async-done(((f32[512,4096]{1,0:T(8,128)}), f32[512,1024]{1,0:T(8,128)}) %reduce-scatter.3.cloned.1.call-update) | async-done | bytes 2097168 | tf_op jit(solution)/shard_map/reduce_scatter | solution.py:83
  146.0 0.0 copy-done.7
  146.0 2.9 add_convert_fusion.1
  148.9 0.0 all-gather.6.cloned.1.call-update
  149.0 0.3 all-gather.8.cloned.1.call-start
  149.2 34.4 %all-gather.6.cloned.1.call-done = bf16[512,4096]{1,0:T(8,128)(2,1)} async-done(((bf16[512,1024]{1,0:T(8,128)(2,1)}), bf16[512,4096]{1,0:T(8,128)(2,1)}) %all-gather.6.cloned.1.call-update) | async-done | bytes 4194320 | tf_op jit(solution)/shard_map/all_gather | solution.py:85
  183.6 3.2 %fusion.4 = f32[512]{0:T(512)S(1)} fusion(bf16[512,4096]{1,0:T(8,128)(2,1)} %all-gather.6.cloned.1.call-done), kind=kLoop, calls=%fused_computation.8 | loop fusion | flops 6290944 | bytes 4196352 | tf_op jit(solution)/shard_map/reduce_sum | solution.py:21
  186.9 0.0 copy-done.14
  186.9 0.0 copy-done.16
  186.9 0.2 copy-done.6
  187.1 1.5 fusion.15
  188.6 0.1 multiply_multiply_fusion.1
  188.7 0.5 copy-done.12
  189.3 2.6 convolution_convert_fusion
  191.9 0.0 copy-start.8
  191.9 1.5 convolution_convert_fusion.2
  193.4 0.0 all-gather.8.cloned.1.call-update
  193.4 0.3 reduce-scatter.5.cloned.1.call-start
  193.7 0.1 iota_compare_fusion
  193.8 0.1 multiply_multiply_fusion
  193.9 2.4 select_convert_fusion
  196.3 26.8 %all-gather.8.cloned.1.call-done = bf16[8,273,256]{2,1,0:T(8,128)(2,1)} async-done(((bf16[2,273,256]{2,1,0:T(8,128)(2,1)}), bf16[8,273,256]{2,1,0:T(8,128)(2,1)}) %all-gather.8.cloned.1.call-update) | async-done | bytes 1118224 | tf_op jit(solution)/shard_map/all_gather | solution.py:105
  223.1 2.0 fusion.26
  225.1 0.0 copy-start.10
  225.1 1.5 bitcast_add_fusion
  226.6 0.0 copy-start.4
  226.7 2.0 fusion.21
  228.7 0.5 multiply_reduce_fusion
  229.2 0.0 copy-done.10
  229.2 0.1 multiply_convert_fusion
  229.4 5.7 %fusion.45 = f32[512,4096]{1,0:T(8,128)} fusion(bf16[512,512]{0,1:T(8,128)(2,1)S(1)} %bitcast.73, bf16[512,4096]{1,0:T(8,128)(2,1)S(1)} %copy-done.4), kind=kOutput, calls=%fused_computation.76 | convolution fusion | flops 2147483648 | bytes 13107200 | tf_op jit(solution)/shard_map/dot_general | solution.py:122
  235.1 0.0 reduce-scatter.5.cloned.1.call-update
  235.1 0.0 copy-start.1
  235.1 71.3 %reduce-scatter.5.cloned.1.call-done = f32[512,1024]{1,0:T(8,128)} async-done(((f32[512,4096]{1,0:T(8,128)}), f32[512,1024]{1,0:T(8,128)}) %reduce-scatter.5.cloned.1.call-update) | async-done | bytes 2097168 | tf_op jit(solution)/shard_map/reduce_scatter | solution.py:123
  306.5 2.9 add_convert_fusion
  (23 shorter events, 0.1 us)
Async XLA Ops:
  6.5 42.8 %copy-start = (bf16[4096,256]{1,0:T(8,128)(2,1)S(1)}, bf16[4096,256]{1,0:T(8,128)(2,1)}, u32[]{:S(2)}) copy-start(bf16[4096,256]{1,0:T(8,128)(2,1)} %param.16) | copy-start | bytes 6291460
  6.5 42.8 %copy-start.15 = (f32[4096]{0:T(1024)S(1)}, f32[4096]{0:T(1024)}, u32[]{:S(2)}) copy-start(f32[4096]{0:T(1024)} %param.13) | copy-start | bytes 49156
  6.5 39.6 %all-gather.4.cloned.1.call-start = ((), (), s32[]{:S(2)}) async-start(), calls=%async_computation.2 | async-start | bytes 5242880 | tf_op jit(solution)/shard_map/all_gather | solution.py:51
  7.3 138.8 %reduce-scatter.3.cloned.1.call-start = ((), (), s32[]{:S(2)}) async-start(), calls=%async_computation.3 | async-start | bytes 10485760 | tf_op jit(solution)/shard_map/reduce_scatter | solution.py:83
  46.1 3.4 %copy-start.5 = (bf16[512,4096]{1,0:T(8,128)(2,1)S(1)}, bf16[512,4096]{1,0:T(8,128)(2,1)}, u32[]{:S(2)}) copy-start(bf16[512,4096]{1,0:T(8,128)(2,1)} %all-gather.4.cloned.1.call-done) | copy-start | bytes 12582916
  49.6 1.6 copy-start.13
  51.2 5.3 %copy-start.11 = (bf16[4096,512]{1,0:T(8,128)(2,1)S(1)}, bf16[4096,512]{1,0:T(8,128)(2,1)}, u32[]{:S(2)}) copy-start(bf16[4096,512]{1,0:T(8,128)(2,1)} %param.14) | copy-start | bytes 12582916
  53.0 6.5 %collective-permute-start = (bf16[64,512]{0,1:T(8,128)(2,1)S(1)}, bf16[64,512]{0,1:T(8,128)(2,1)S(1)}, u32[]{:S(2)}, u32[]{:S(2)}) collective-permute-start(bf16[64,512]{0,1:T(8,128)(2,1)S(1)} %pad_maximum_fusion), channel_id=1, source_target_pairs={{0,4},{4,8},{8,12},{1,5},{5,9},{9,13},{2,6},{6,10},{10,14},{3,7},{... | collective-permute-start | bytes 196616 | tf_op jit(solution)/shard_map/ppermute | solution.py:16
  63.8 3.6 %copy-start.3 = (bf16[512,4096]{1,0:T(8,128)(2,1)S(1)}, bf16[512,4096]{1,0:T(8,128)(2,1)}, u32[]{:S(2)}) copy-start(bf16[512,4096]{1,0:T(8,128)(2,1)} %param.17) | copy-start | bytes 12582916
  73.1 72.9 %copy-start.7 = (bf16[512,1024]{1,0:T(8,128)(2,1)S(1)}, bf16[512,1024]{1,0:T(8,128)(2,1)}, u32[]{:S(2)}) copy-start(bf16[512,1024]{1,0:T(8,128)(2,1)} %param.12) | copy-start | bytes 3145732
  73.2 113.7 %copy-start.14 = (bf16[4096,64]{0,1:T(8,128)(2,1)S(1)}, bf16[4096,64]{0,1:T(8,128)(2,1)}, u32[]{:S(2)}) copy-start(bf16[4096,64]{0,1:T(8,128)(2,1)} %param.19) | copy-start | bytes 1572868
  73.2 113.7 %copy-start.16 = (f32[4096]{0:T(1024)S(1)}, f32[4096]{0:T(1024)}, u32[]{:S(2)}) copy-start(f32[4096]{0:T(1024)} %param.18) | copy-start | bytes 49156
  73.2 110.4 %all-gather.6.cloned.1.call-start = ((), (), s32[]{:S(2)}) async-start(), calls=%async_computation.4 | async-start | bytes 5242880 | tf_op jit(solution)/shard_map/all_gather | solution.py:85
  149.0 74.2 %all-gather.8.cloned.1.call-start = ((), (), s32[]{:S(2)}) async-start(), calls=%async_computation.5 | async-start | bytes 1433600 | tf_op jit(solution)/shard_map/all_gather | solution.py:105
  183.6 3.4 %copy-start.6 = (bf16[512,4096]{1,0:T(8,128)(2,1)S(1)}, bf16[512,4096]{1,0:T(8,128)(2,1)}, u32[]{:S(2)}) copy-start(bf16[512,4096]{1,0:T(8,128)(2,1)} %all-gather.6.cloned.1.call-done) | copy-start | bytes 12582916
  187.1 2.2 copy-start.12
  191.9 31.3 %copy-start.8 = (bf16[512,512]{0,1:T(8,128)(2,1)}, bf16[512,512]{0,1:T(8,128)(2,1)S(1)}, u32[]{:S(2)}) copy-start(bf16[512,512]{0,1:T(8,128)(2,1)S(1)} %convolution_convert_fusion) | copy-start | bytes 1572868
  193.4 113.0 %reduce-scatter.5.cloned.1.call-start = ((), (), s32[]{:S(2)}) async-start(), calls=%async_computation.6 | async-start | bytes 10485760 | tf_op jit(solution)/shard_map/reduce_scatter | solution.py:123
  225.1 3.6 %copy-start.9 = (bf16[512,512]{0,1:T(8,128)(2,1)S(1)}, bf16[512,512]{0,1:T(8,128)(2,1)}, u32[]{:S(2)}) copy-start(bf16[512,512]{0,1:T(8,128)(2,1)} %copy-done.8) | copy-start | bytes 1572868
  225.1 4.1 %copy-start.10 = (f32[2,256]{1,0:T(2,128)S(1)}, f32[2,256]{1,0:T(2,128)}, u32[]{:S(2)}) copy-start(f32[2,256]{1,0:T(2,128)} %param.21) | copy-start | bytes 6148
  226.6 2.7 copy-start.4
  235.1 71.4 %copy-start.2 = (bf16[512,1024]{1,0:T(8,128)(2,1)S(1)}, bf16[512,1024]{1,0:T(8,128)(2,1)}, u32[]{:S(2)}) copy-start(bf16[512,1024]{1,0:T(8,128)(2,1)} %add_convert_fusion.1) | copy-start | bytes 3145732
  235.1 74.3 %copy-start.1 = (bf16[4096,256]{1,0:T(8,128)(2,1)S(1)}, bf16[4096,256]{1,0:T(8,128)(2,1)}, u32[]{:S(2)}) copy-start(bf16[4096,256]{1,0:T(8,128)(2,1)} %param.16) | copy-start | bytes 6291460
Sparse Core Ops, SparseCore 0:
  8.9 37.1 all-gather.3
  73.3 72.6 reduce-scatter.2
  149.1 34.4 all-gather.5
  193.5 29.5 all-gather.7
  235.2 71.1 reduce-scatter.4
where the time goes:
time: 316 us
  waiting for transfers between devices  245 us (78%)
  matrix products  36.6 us (12%)
  other arithmetic  15.1 us (5%)
  between operations  13.5 us (4%)
  starting transfers between devices  4.22 us (1%)
    reduce_scatter x1, waiting for transfers between devices, body(): lax.psum_scatter(terms, 'head', scatter_dimension=1, tiled=True)  72.8 us
    reduce_scatter x1, waiting for transfers between devices, body(): lax.psum_scatter(lin_terms, 'head', scatter_dimension=1, tiled=True)  71.3 us
    all_gather x1, waiting for transfers between devices, body(): whole = lax.all_gather(hidden_in, 'head', axis=1, tiled=True)  38.4 us
    all_gather x1, waiting for transfers between devices, body(): after_whole = lax.all_gather(after_window, 'head', axis=1, tiled=True)  34.4 us
    all_gather x1, waiting for transfers between devices, body(): lax.all_gather(local_state.astype(jnp.bfloat16), 'ctx', axis=0, tiled=True)  26.8 us
    reduce_sum x2, other arithmetic, norm_rows(): scale = lax.rsqrt(jnp.mean(wide * wide, axis=-1, keepdims=True) + 1e-05)  6.46 us
  transfers between devices with their start and end apart: 6, of which 6 were waited for; matrix products, arithmetic and copies ran while one was open for 2% of the time, Pallas kernels for 0%

commit v1 on v0

--- a/solution.py
+++ b/solution.py
@@ -8,6 +8,24 @@
 WINDOW = 64
 FEAT = 16
 VDIM = 256
+
+
+def gather_around(shard, axis, dim):
+    ways, here, step = (lax.axis_size(axis), lax.axis_index(axis), shard.shape[dim])
+    shape = [n * ways if d == dim else n for d, n in enumerate(shard.shape)]
+    full = lax.dynamic_update_slice_in_dim(
+        jnp.zeros(shape, shard.dtype), shard, here * step, axis=dim
+    )
+    going_up = going_down = shard
+    for far in range(1, ways // 2 + 1):
+        going_up = lax.ppermute(going_up, axis, [(d, (d + 1) % ways) for d in range(ways)])
+        full = lax.dynamic_update_slice_in_dim(full, going_up, (here - far) % ways * step, axis=dim)
+        if 2 * far < ways:
+            going_down = lax.ppermute(going_down, axis, [(d, (d - 1) % ways) for d in range(ways)])
+            full = lax.dynamic_update_slice_in_dim(
+                full, going_down, (here + far) % ways * step, axis=dim
+            )
+    return full
 
 
 def from_behind(value, axis, by):
@@ -102,7 +120,7 @@
     )
     ctx_count = lax.axis_size("ctx")
     every = (
-        lax.all_gather(local_state.astype(jnp.bfloat16), "ctx", axis=0, tiled=True)
+        gather_around(local_state.astype(jnp.bfloat16), "ctx", 0)
         .astype(local_state.dtype)
         .reshape((ctx_count,) + local_state.shape)
     )

time: 316 us -> 306 us (0.968)
  waiting for transfers between devices: 245 us -> 233 us
  starting transfers between devices: 4.22 us -> 7.8 us
    all_gather x1 -> x0, waiting for transfers between devices: 26.8 us -> none  [body(): lax.all_gather(local_state.astype(jnp.bfloat16), 'ctx', axis=0, tiled=True)]
    ppermute x0 -> x3, waiting for transfers between devices: none -> 16.5 us  [the longest x2 11.4 us: gather_around(): lax.ppermute(going_up, axis, [(d, (d + 1) % ways) for d in range(ways)])]
    ppermute x0 -> x3, starting transfers between devices: none -> 3.88 us  [the longest x1 2.39 us: gather_around(): lax.ppermute(going_down, axis, [(d, (d - 1) % ways) for d in range(ways)])]
  transfers between devices with their start and end apart: 6 -> 8, of which waited for: 6 -> 8; matrix products, arithmetic and copies ran while one was open for 2% -> 2% of each run, Pallas kernels for 0% -> 0%
where the time goes in v1:
time: 306 us
  waiting for transfers between devices  233 us (76%)
  matrix products  34.7 us (11%)
  other arithmetic  14 us (5%)
  between operations  13.6 us (4%)
  starting transfers between devices  7.8 us (3%)
    reduce_scatter x1, waiting for transfers between devices, body(): lax.psum_scatter(terms, 'head', scatter_dimension=1, tiled=True)  72.8 us
    reduce_scatter x1, waiting for transfers between devices, body(): lax.psum_scatter(lin_terms, 'head', scatter_dimension=1, tiled=True)  70 us
    all_gather x1, waiting for transfers between devices, body(): whole = lax.all_gather(hidden_in, 'head', axis=1, tiled=True)  38.4 us
    all_gather x1, waiting for transfers between devices, body(): after_whole = lax.all_gather(after_window, 'head', axis=1, tiled=True)  34.4 us
    ppermute x2, waiting for transfers between devices, gather_around(): lax.ppermute(going_up, axis, [(d, (d + 1) % ways) for d in range(ways)])  11.4 us
    reduce_sum x2, other arithmetic, norm_rows(): scale = lax.rsqrt(jnp.mean(wide * wide, axis=-1, keepdims=True) + 1e-05)  6.46 us
  transfers between devices with their start and end apart: 8, of which 8 were waited for; matrix products, arithmetic and copies ran while one was open for 2% of the time, Pallas kernels for 0%

profile of v1, /device:TPU:0, one launch (start us, length us, event | category | flops | bytes accessed | tf_op | source)
XLA Modules:
  0.0 306.0 jit_solution(17949677367431826794)
XLA Ops:
  6.5 0.0 copy-start
  6.5 0.0 all-gather.3.cloned.1.call-start
  6.5 0.7 all-gather.3.cloned.1.call-update
  7.3 0.0 reduce-scatter.3.cloned.1.call-start
  7.4 0.3 and_and_fusion
  7.7 38.4 %all-gather.3.cloned.1.call-done = bf16[512,4096]{1,0:T(8,128)(2,1)} async-done(((bf16[512,1024]{1,0:T(8,128)(2,1)}), bf16[512,4096]{1,0:T(8,128)(2,1)}) %all-gather.3.cloned.1.call-update) | async-done | bytes 4194320 | tf_op jit(solution)/shard_map/all_gather | solution.py:69
  46.1 3.2 %fusion.1 = f32[512]{0:T(512)S(1)} fusion(bf16[512,4096]{1,0:T(8,128)(2,1)} %all-gather.3.cloned.1.call-done), kind=kLoop, calls=%fused_computation.5 | loop fusion | flops 6290944 | bytes 4196352 | tf_op jit(solution)/shard_map/reduce_sum | solution.py:39
  49.4 0.0 copy-done
  49.4 0.2 copy-done.5
  49.6 1.6 convolution_convert_fusion.4
  51.2 0.0 copy-start.12
  51.2 1.6 convolution_convert_fusion.3
  52.9 0.1 pad_maximum_fusion
  53.0 3.6 %collective-permute-start = (bf16[64,512]{0,1:T(8,128)(2,1)S(1)}, bf16[64,512]{0,1:T(8,128)(2,1)S(1)}, u32[]{:S(2)}, u32[]{:S(2)}) collective-permute-start(bf16[64,512]{0,1:T(8,128)(2,1)S(1)} %pad_maximum_fusion), channel_id=1, source_target_pairs={{0,4},{4,8},{8,12},{1,5},{5,9},{9,13},{2,6},{6,10},{10,14},{3,7},{... | collective-permute-start | bytes 196616 | tf_op jit(solution)/shard_map/ppermute | solution.py:34
  56.6 2.6 convolution_convert_fusion.1
  59.2 0.3 collective-permute-done
  59.5 0.3 maximum_maximum_fusion
  59.8 0.1 fusion.42
  59.9 3.9 %fusion.43 = (f32[2,2,512]{2,1,0:T(2,128)S(1)}, f32[2,2,512,576]{2,3,1,0:T(8,128)}) fusion(pred[512,576]{0,1:T(8,128)(4,1)S(1)} %and_and_fusion, bf16[576,2,128,1]{0,2,3,1:T(8,128)(2,1)S(1)} %bitcast.83, bf16[512,2,2,128]{0,3,2,1:T(8,128)(2,1)S(1)} %bitcast.84), kind=kOutput, calls=%fused_computation.78 | convolution fusion | flops 306709056 | bytes 5840896 | tf_op jit(solution)/shard_map/sub | solution.py:96
  63.8 3.1 %fusion.13 = bf16[2,128,2,512]{3,1,2,0:T(8,128)(2,1)S(1)} fusion(bf16[576,2,128,1]{0,2,3,1:T(8,128)(2,1)S(1)} %bitcast.82, f32[2,2,512,576]{2,3,1,0:T(8,128)} %get-tuple-element.12, f32[2,2,512]{2,1,0:T(2,128)S(1)} %get-tuple-element.11), kind=kOutput, calls=%fused_computation.26 | convolution fusion | flops 304611328 | bytes 5545984 | tf_op jit(solution)/shard_map/kgts,skd->tkgd/dot_general | solution.py:98
  66.9 0.5 copy-done.3
  67.4 5.7 %fusion.44 = f32[512,4096]{1,0:T(8,128)} fusion(bf16[512,512]{0,1:T(8,128)(2,1)S(1)} %bitcast.78, bf16[512,4096]{1,0:T(8,128)(2,1)S(1)} %copy-done.3), kind=kOutput, calls=%fused_computation.79 | convolution fusion | flops 2147483648 | bytes 13107200 | tf_op jit(solution)/shard_map/dot_general | solution.py:100
  73.1 0.0 reduce-scatter.3.cloned.1.call-update
  73.2 0.0 copy-start.15
  73.2 0.0 copy-start.17
  73.2 0.0 all-gather.5.cloned.1.call-start
  73.2 72.8 %reduce-scatter.3.cloned.1.call-done = f32[512,1024]{1,0:T(8,128)} async-done(((f32[512,4096]{1,0:T(8,128)}), f32[512,1024]{1,0:T(8,128)}) %reduce-scatter.3.cloned.1.call-update) | async-done | bytes 2097168 | tf_op jit(solution)/shard_map/reduce_scatter | solution.py:101
  146.0 2.9 add_convert_fusion.1
  148.9 0.0 all-gather.5.cloned.1.call-update
  149.0 0.3 reduce-scatter.5.cloned.1.call-start
  149.3 34.4 %all-gather.5.cloned.1.call-done = bf16[512,4096]{1,0:T(8,128)(2,1)} async-done(((bf16[512,1024]{1,0:T(8,128)(2,1)}), bf16[512,4096]{1,0:T(8,128)(2,1)}) %all-gather.5.cloned.1.call-update) | async-done | bytes 4194320 | tf_op jit(solution)/shard_map/all_gather | solution.py:103
  183.6 3.2 %fusion.4 = f32[512]{0:T(512)S(1)} fusion(bf16[512,4096]{1,0:T(8,128)(2,1)} %all-gather.5.cloned.1.call-done), kind=kLoop, calls=%fused_computation.8 | loop fusion | flops 6290944 | bytes 4196352 | tf_op jit(solution)/shard_map/reduce_sum | solution.py:39
  186.9 0.2 copy-done.6
  187.1 1.5 fusion.15
  188.6 0.1 multiply_multiply_fusion.1
  188.7 0.5 copy-done.13
  189.2 2.6 convolution_convert_fusion
  191.9 0.1 broadcast_in_dim.20
  191.9 0.8 constant_dynamic-update-slice_fusion.3
  192.7 1.0 copy-done.8
  193.8 1.5 collective-permute-start.1
  195.3 0.1 iota_compare_fusion
  195.4 0.0 copy-start.10
  195.4 2.4 collective-permute-start.2
  197.8 2.3 select_convert_fusion
  200.2 5.1 %collective-permute-done.1 = bf16[2,273,256]{2,1,0:T(8,128)(2,1)S(1)} collective-permute-done((bf16[2,273,256]{2,1,0:T(8,128)(2,1)S(1)}, bf16[2,273,256]{2,1,0:T(8,128)(2,1)S(1)}, u32[]{:S(2)}, u32[]{:S(2)}) %collective-permute-start.1) | collective-permute-done | bytes 279584 | tf_op jit(solution)/shard_map/ppermute | solution.py:21
  205.3 0.0 collective-permute-start.3
  205.3 0.1 multiply_multiply_fusion
  205.4 0.0 copy-done.9
  205.5 5.1 %collective-permute-done.2 = bf16[2,273,256]{2,1,0:T(8,128)(2,1)S(1)} collective-permute-done((bf16[2,273,256]{2,1,0:T(8,128)(2,1)S(1)}, bf16[2,273,256]{2,1,0:T(8,128)(2,1)S(1)}, u32[]{:S(2)}, u32[]{:S(2)}) %collective-permute-start.2) | collective-permute-done | bytes 279584 | tf_op jit(solution)/shard_map/ppermute | solution.py:24
  210.6 6.3 %collective-permute-done.3 = bf16[2,273,256]{2,1,0:T(8,128)(2,1)S(1)} collective-permute-done((bf16[2,273,256]{2,1,0:T(8,128)(2,1)S(1)}, bf16[2,273,256]{2,1,0:T(8,128)(2,1)S(1)}, u32[]{:S(2)}, u32[]{:S(2)}) %collective-permute-start.3) | collective-permute-done | bytes 279584 | tf_op jit(solution)/shard_map/ppermute | solution.py:21
  216.9 0.7 fusion.26
  217.7 0.0 copy-done.10
  217.7 0.0 copy-start.11
  217.7 0.4 bitcast_add_fusion
  218.1 0.0 copy-start.4
  218.1 2.0 fusion.21
  220.1 0.5 multiply_reduce_fusion
  220.6 0.1 multiply_convert_fusion
  220.8 5.7 %fusion.45 = f32[512,4096]{1,0:T(8,128)} fusion(bf16[512,512]{0,1:T(8,128)(2,1)S(1)} %bitcast.74, bf16[512,4096]{1,0:T(8,128)(2,1)S(1)} %copy-done.4), kind=kOutput, calls=%fused_computation.80 | convolution fusion | flops 2147483648 | bytes 13107200 | tf_op jit(solution)/shard_map/dot_general | solution.py:140
  226.5 0.0 reduce-scatter.5.cloned.1.call-update
  226.5 0.0 copy-start.1
  226.5 70.0 %reduce-scatter.5.cloned.1.call-done = f32[512,1024]{1,0:T(8,128)} async-done(((f32[512,4096]{1,0:T(8,128)}), f32[512,1024]{1,0:T(8,128)}) %reduce-scatter.5.cloned.1.call-update) | async-done | bytes 2097168 | tf_op jit(solution)/shard_map/reduce_scatter | solution.py:141
  296.6 2.9 add_convert_fusion
  (32 shorter events, 0.2 us)
Async XLA Ops:
  6.5 42.8 %copy-start = (bf16[4096,256]{1,0:T(8,128)(2,1)S(1)}, bf16[4096,256]{1,0:T(8,128)(2,1)}, u32[]{:S(2)}) copy-start(bf16[4096,256]{1,0:T(8,128)(2,1)} %param.15) | copy-start | bytes 6291460
  6.5 42.8 %copy-start.16 = (f32[4096]{0:T(1024)S(1)}, f32[4096]{0:T(1024)}, u32[]{:S(2)}) copy-start(f32[4096]{0:T(1024)} %param.13) | copy-start | bytes 49156
  6.5 39.6 %all-gather.3.cloned.1.call-start = ((), (), s32[]{:S(2)}) async-start(), calls=%async_computation.2 | async-start | bytes 5242880 | tf_op jit(solution)/shard_map/all_gather | solution.py:69
  7.3 138.8 %reduce-scatter.3.cloned.1.call-start = ((), (), s32[]{:S(2)}) async-start(), calls=%async_computation.3 | async-start | bytes 10485760 | tf_op jit(solution)/shard_map/reduce_scatter | solution.py:101
  46.1 3.4 %copy-start.5 = (bf16[512,4096]{1,0:T(8,128)(2,1)S(1)}, bf16[512,4096]{1,0:T(8,128)(2,1)}, u32[]{:S(2)}) copy-start(bf16[512,4096]{1,0:T(8,128)(2,1)} %all-gather.3.cloned.1.call-done) | copy-start | bytes 12582916
  49.6 1.6 copy-start.14
  51.2 5.3 %copy-start.12 = (bf16[4096,512]{1,0:T(8,128)(2,1)S(1)}, bf16[4096,512]{1,0:T(8,128)(2,1)}, u32[]{:S(2)}) copy-start(bf16[4096,512]{1,0:T(8,128)(2,1)} %param.14) | copy-start | bytes 12582916
  53.0 6.5 %collective-permute-start = (bf16[64,512]{0,1:T(8,128)(2,1)S(1)}, bf16[64,512]{0,1:T(8,128)(2,1)S(1)}, u32[]{:S(2)}, u32[]{:S(2)}) collective-permute-start(bf16[64,512]{0,1:T(8,128)(2,1)S(1)} %pad_maximum_fusion), channel_id=1, source_target_pairs={{0,4},{4,8},{8,12},{1,5},{5,9},{9,13},{2,6},{6,10},{10,14},{3,7},{... | collective-permute-start | bytes 196616 | tf_op jit(solution)/shard_map/ppermute | solution.py:34
  63.8 3.6 %copy-start.3 = (bf16[512,4096]{1,0:T(8,128)(2,1)S(1)}, bf16[512,4096]{1,0:T(8,128)(2,1)}, u32[]{:S(2)}) copy-start(bf16[512,4096]{1,0:T(8,128)(2,1)} %param.17) | copy-start | bytes 12582916
  73.1 72.9 %copy-start.7 = (bf16[512,1024]{1,0:T(8,128)(2,1)S(1)}, bf16[512,1024]{1,0:T(8,128)(2,1)}, u32[]{:S(2)}) copy-start(bf16[512,1024]{1,0:T(8,128)(2,1)} %param.12) | copy-start | bytes 3145732
  73.2 113.7 %copy-start.15 = (bf16[4096,64]{0,1:T(8,128)(2,1)S(1)}, bf16[4096,64]{0,1:T(8,128)(2,1)}, u32[]{:S(2)}) copy-start(bf16[4096,64]{0,1:T(8,128)(2,1)} %param.19) | copy-start | bytes 1572868
  73.2 113.7 %copy-start.17 = (f32[4096]{0:T(1024)S(1)}, f32[4096]{0:T(1024)}, u32[]{:S(2)}) copy-start(f32[4096]{0:T(1024)} %param.18) | copy-start | bytes 49156
  73.2 110.4 %all-gather.5.cloned.1.call-start = ((), (), s32[]{:S(2)}) async-start(), calls=%async_computation.4 | async-start | bytes 5242880 | tf_op jit(solution)/shard_map/all_gather | solution.py:103
  149.0 147.6 %reduce-scatter.5.cloned.1.call-start = ((), (), s32[]{:S(2)}) async-start(), calls=%async_computation.5 | async-start | bytes 10485760 | tf_op jit(solution)/shard_map/reduce_scatter | solution.py:141
  183.6 3.4 %copy-start.6 = (bf16[512,4096]{1,0:T(8,128)(2,1)S(1)}, bf16[512,4096]{1,0:T(8,128)(2,1)}, u32[]{:S(2)}) copy-start(bf16[512,4096]{1,0:T(8,128)(2,1)} %all-gather.5.cloned.1.call-done) | copy-start | bytes 12582916
  187.1 2.2 copy-start.13
  192.7 1.0 copy-start.8
  193.8 11.5 %collective-permute-start.1 = (bf16[2,273,256]{2,1,0:T(8,128)(2,1)S(1)}, bf16[2,273,256]{2,1,0:T(8,128)(2,1)S(1)}, u32[]{:S(2)}, u32[]{:S(2)}) collective-permute-start(bf16[2,273,256]{2,1,0:T(8,128)(2,1)S(1)} %get-tuple-element.14), channel_id=1, source_target_pairs={{0,4},{4,8},{8,12},{12,0},{1,5},{5,9},{9,13},{13,1},{2,6},{6,10},{... | collective-permute-start | bytes 838664 | tf_op jit(solution)/shard_map/ppermute | solution.py:21
  195.4 10.0 %copy-start.9 = (bf16[8,273,256]{2,1,0:T(8,128)(2,1)S(1)}, bf16[8,273,256]{2,1,0:T(8,128)(2,1)}, u32[]{:S(2)}) copy-start(bf16[8,273,256]{2,1,0:T(8,128)(2,1)} %copy-done.8) | copy-start | bytes 3354628
  195.4 22.2 %copy-start.10 = (f32[2,273,256]{2,0,1:T(2,128)S(1)}, f32[2,273,256]{2,0,1:T(2,128)}, u32[]{:S(2)}) copy-start(f32[2,273,256]{2,0,1:T(2,128)} %param.23) | copy-start | bytes 1677316
  195.4 15.2 %collective-permute-start.2 = (bf16[2,273,256]{2,1,0:T(8,128)(2,1)S(1)}, bf16[2,273,256]{2,1,0:T(8,128)(2,1)S(1)}, u32[]{:S(2)}, u32[]{:S(2)}) collective-permute-start(bf16[2,273,256]{2,1,0:T(8,128)(2,1)S(1)} %get-tuple-element.14), channel_id=1, source_target_pairs={{0,12},{4,0},{8,4},{12,8},{1,13},{5,1},{9,5},{13,9},{2,14},{6,2},{... | collective-permute-start | bytes 838664 | tf_op jit(solution)/shard_map/ppermute | solution.py:24
  205.3 11.6 %collective-permute-start.3 = (bf16[2,273,256]{2,1,0:T(8,128)(2,1)S(1)}, bf16[2,273,256]{2,1,0:T(8,128)(2,1)S(1)}, u32[]{:S(2)}, u32[]{:S(2)}) collective-permute-start(bf16[2,273,256]{2,1,0:T(8,128)(2,1)S(1)} %collective-permute-done.1), channel_id=1, source_target_pairs={{0,4},{4,8},{8,12},{12,0},{1,5},{5,9},{9,13},{13,1},{2,6},{6,10},{... | collective-permute-start | bytes 838664 | tf_op jit(solution)/shard_map/ppermute | solution.py:21
  217.7 3.0 copy-start.11
  218.1 2.7 copy-start.4
  226.5 70.0 %copy-start.2 = (bf16[512,1024]{1,0:T(8,128)(2,1)S(1)}, bf16[512,1024]{1,0:T(8,128)(2,1)}, u32[]{:S(2)}) copy-start(bf16[512,1024]{1,0:T(8,128)(2,1)} %add_convert_fusion.1) | copy-start | bytes 3145732
  226.5 72.9 %copy-start.1 = (bf16[4096,256]{1,0:T(8,128)(2,1)S(1)}, bf16[4096,256]{1,0:T(8,128)(2,1)}, u32[]{:S(2)}) copy-start(bf16[4096,256]{1,0:T(8,128)(2,1)} %param.15) | copy-start | bytes 6291460
Sparse Core Ops, SparseCore 0:
  8.9 37.1 all-gather.2
  73.3 72.7 reduce-scatter.2
  149.1 34.4 all-gather.4
  226.7 69.8 reduce-scatter.4
